TPU v7x, 128 devices: a whole 4x4x4 slice. The times are simulated.
128 devices in a mesh: wide: 16 (over z, y), col: 8 (over x, core).
Axes of the slice: x: 4, y: 4, z: 4, core: 2. Of those that a mesh axis runs over, the one named last changes fastest.
Arguments:
- z_root: float32 [512, 16384], P('col', 'wide'), may hold values from -6 to 6
- z_child: float32 [512, 2, 8192], P('col', None, 'wide'), may hold values from -6 to 6
- z_grand: float32 [512, 4, 4096], P('col', None, 'wide'), may hold values from -6 to 6
- inv_root: float32 [16384, 16384], P('wide', 'col'), as said below
- inv_child: float32 [2, 8192, 8192], P(None, 'wide', 'col'), as said below
- inv_grand: float32 [4, 4096, 4096], P(None, 'wide', 'col'), as said below
- panel_child: float32 [2, 4096, 8192], P(None, 'col', 'wide'), may hold values from -0.046875 to 0.046875
- panel_grand: float32 [4, 2048, 4096], P(None, 'col', 'wide'), may hold values from -0.0625 to 0.0625
- anc_child: int32 [2, 32], P(None, 'col'), may hold values from 0 to 127, as said below
- anc_grand: int32 [4, 16], P(None, 'col'), may hold values from 0 to 255, as said below
Outputs:
- x_root: float32 [512, 16384], P('wide', 'col')
- x_child: float32 [512, 2, 8192], P('wide', None, 'col')
- x_grand: float32 [512, 4, 4096], P('wide', None, 'col')
Inputs may be any that keep to these rules, and one draw needn't show every extreme that they name: inv_root is lower triangular with a positive diagonal (entries above the diagonal are zero). Each inv_child[k] is lower triangular with a positive diagonal. Each inv_grand[g] is lower triangular with a positive diagonal. `anc_child`: each row lists distinct blocks in rising order and always names block 0 and block 127. `anc_grand`: row g lists 2048 // 256 distinct root blocks in rising order, block 0 and block 127 among them, then as many distinct blocks of child g // 2 (numbered 16384 // 128 + (g // 2) * 64 onwards) in rising order, its first and its last among them.
All inputs are finite; a program needn't handle non-finite values.
Results may differ from a plain program's by a relative error of at most 0.000096.
Values sent between devices are 32-bit elements; how exact they have to be, the bound alone decides.
No kernel may reach another device: no remote copies, remote signals or barrier semaphores. Data moves between devices by JAX's collectives and lax.ppermute only.
A program may use at most 128 MiB of HBM per device.

v0:
```python
import jax
import jax.numpy as jnp
from jax import lax
from jax.sharding import PartitionSpec as P

BLK = 128
PRECISE = lax.Precision.HIGHEST


def pick_blocks(source_rows, blocks):
    leading = source_rows.shape[0]
    tiled = source_rows.reshape(leading, source_rows.shape[1] // BLK, BLK)
    selected = jnp.take(tiled, blocks.reshape(-1), axis=1)
    return selected.reshape(leading, blocks.shape[0], blocks.shape[1] * BLK)


def spread_rhs(local_part):
    return lax.all_gather(local_part, "col", axis=0, tiled=True)


def solve_terms(right_rows, inverse):
    return lax.psum_scatter(
        jnp.einsum(
            "ski,kij->skj",
            right_rows,
            inverse,
            precision=PRECISE,
            preferred_element_type=jnp.float32,
        ),
        "wide",
        scatter_dimension=0,
        tiled=True,
    )


def spread_solved(solved_local):
    gathered = lax.all_gather(solved_local, "col", axis=2, tiled=True)
    return gathered.reshape(gathered.shape[0], -1)


def fetch_ancestors(source_rows, blocks):
    return lax.all_gather(pick_blocks(source_rows, blocks), "wide", axis=0, tiled=True)


def finish_level(z_local, inverse, partial_value):
    summed = lax.psum(partial_value, "col")
    right_side = spread_rhs(z_local) - summed
    solved = solve_terms(right_side, inverse)
    return solved


def per_device(
    z_root,
    z_child,
    z_grand,
    inv_root,
    inv_child,
    inv_grand,
    panel_child,
    panel_grand,
    anc_child,
    anc_grand,
):
    root_right = spread_rhs(z_root[:, None, :])
    root_solved = solve_terms(root_right, inv_root[None])
    x_root = root_solved[:, 0, :]
    root_rows = spread_solved(root_solved)
    near_rows = fetch_ancestors(root_rows, anc_child)
    partial_value = jnp.einsum(
        "ska,kaj->skj",
        near_rows,
        panel_child,
        precision=PRECISE,
        preferred_element_type=jnp.float32,
    )
    x_child = finish_level(z_child, inv_child, partial_value)
    child_rows = spread_solved(x_child)
    solved_all = jnp.concatenate([root_rows, child_rows], axis=1)
    far_rows = fetch_ancestors(solved_all, anc_grand)
    partial_grand = jnp.einsum(
        "sga,gaj->sgj", far_rows, panel_grand, precision=PRECISE, preferred_element_type=jnp.float32
    )
    x_grand = finish_level(z_grand, inv_grand, partial_grand)
    return (x_root, x_child, x_grand)


def solution(mesh):
    in_specs = (
        P("col", "wide"),
        P("col", None, "wide"),
        P("col", None, "wide"),
        P("wide", "col"),
        P(None, "wide", "col"),
        P(None, "wide", "col"),
        P(None, "col", "wide"),
        P(None, "col", "wide"),
        P(None, "col"),
        P(None, "col"),
    )
    out_specs = (P("wide", "col"), P("wide", None, "col"), P("wide", None, "col"))
    return jax.shard_map(
        per_device, mesh=mesh, in_specs=in_specs, out_specs=out_specs, check_vma=False
    )
```

profile of v0, /device:TPU:0, one launch (start us, length us, event | category | flops | bytes accessed | tf_op | source)
XLA Modules:
  0.0 726.2 jit_solution(2255232434404925078)
XLA Ops:
  8.0 29.4 %all-gather.21.cloned.1.call-done = f32[512,1024]{1,0:T(8,128)} async-done(((f32[64,1024]{1,0:T(8,128)}), f32[512,1024]{1,0:T(8,128)}) %all-gather.21.cloned.1.call-update) | async-done | bytes 2097168 | tf_op jit(solution)/shard_map/all_gather | solution.py:18
  37.4 30.4 %convolution_bitcast_fusion = f32[512,1,2048]{0,2,1:T(8,128)} fusion(f32[1024,2048]{1,0:T(8,128)} %param.13, f32[512,1024]{1,0:T(8,128)} %all-gather.21.cloned.1.call-done), kind=kOutput, calls=%fused_computation.3 | convolution fusion | flops 12884901888 | bytes 14680064 | tf_op jit(solution)/shard_map/ski,kij->skj/dot_general | solution.py:23
  67.8 11.0 %copy.75 = f32[512,1,2048]{2,1,0:T(1,128)} copy(f32[512,1,2048]{0,2,1:T(8,128)} %convolution_bitcast_fusion) | data formatting | bytes 8388608 | tf_op jit(solution)/shard_map/ski,kij->skj/transpose | solution.py:23
  80.7 102.2 %all-reduce.9.cloned.1.call-done = f32[512,1,2048]{2,1,0:T(1,128)} async-done(((f32[512,1,2048]{2,1,0:T(1,128)}), f32[512,1,2048]{2,1,0:T(1,128)}) %all-reduce.9.cloned.1.call-update) | async-done | bytes 4194320
  184.9 25.1 %all-gather.11.cloned.1.call-done = f32[32,1,16384]{2,1,0:T(1,128)} async-done(((f32[32,1,2048]{2,1,0:T(1,128)}), f32[32,1,16384]{2,1,0:T(1,128)}) %all-gather.11.cloned.1.call-update) | async-done | bytes 2097168 | tf_op jit(solution)/shard_map/all_gather | solution.py:37
  210.0 4.2 copy.77
  218.2 44.9 %all-gather.13.cloned.1.call-done = f32[512,2,512]{2,0,1:T(8,128)} async-done(((f32[32,2,512]{2,0,1:T(8,128)}), f32[512,2,512]{2,0,1:T(8,128)}) %all-gather.13.cloned.1.call-update) | async-done | bytes 2097168 | tf_op jit(solution)/shard_map/all_gather | solution.py:42
  263.0 7.0 convolution_bitcast_fusion.4
  270.1 19.4 %all-gather.9.cloned.1.call-done = f32[512,2,512]{2,0,1:T(8,128)} async-done(((f32[64,2,512]{2,0,1:T(8,128)}), f32[512,2,512]{2,0,1:T(8,128)}) %all-gather.9.cloned.1.call-update) | async-done | bytes 2097168 | tf_op jit(solution)/shard_map/all_gather | solution.py:18
  289.6 68.2 %all-reduce.5.cloned.1.call-done = f32[512,2,512]{2,0,1:T(8,128)} async-done(((f32[512,2,512]{2,0,1:T(8,128)}), f32[512,2,512]{2,0,1:T(8,128)}) %all-reduce.5.cloned.1.call-update) | async-done | bytes 2097168 | tf_op jit(solution)/shard_map/psum | solution.py:46
  357.8 12.2 %convolution_bitcast_fusion.2 = f32[512,2,1024]{2,0,1:T(8,128)} fusion(f32[2,512,1024]{2,1,0:T(8,128)} %param.14, f32[512,2,512]{2,0,1:T(8,128)} %all-gather.9.cloned.1.call-done, f32[512,2,512]{2,0,1:T(8,128)} %all-reduce.5.cloned.1.call-done), kind=kOutput, calls=%fused_computation.5 | convolution fusion | flops 6442975232 | bytes 12582912 | tf_op jit(solution)/shard_map/ski,kij->skj/dot_general | solution.py:23
  370.1 77.5 %reduce-scatter.3.cloned.1.call-done = f32[32,2,1024]{2,0,1:T(8,128)} async-done(((f32[512,2,1024]{2,0,1:T(8,128)}), f32[32,2,1024]{2,0,1:T(8,128)}) %reduce-scatter.3.cloned.1.call-update) | async-done | bytes 262160 | tf_op jit(solution)/shard_map/reduce_scatter | solution.py:22
  447.9 25.8 %all-gather.17.cloned.1.call-done = f32[32,2,8192]{2,0,1:T(8,128)} async-done(((f32[32,2,1024]{2,0,1:T(8,128)}), f32[32,2,8192]{2,0,1:T(8,128)}) %all-gather.17.cloned.1.call-update) | async-done | bytes 2097168 | tf_op jit(solution)/shard_map/all_gather | solution.py:37
  473.7 4.6 copy.81
  478.3 4.0 concatenate.6
  482.3 3.0 copy.83
  485.3 2.4 pad_maximum_fusion
  487.7 2.8 gather_fusion.1
  493.2 43.9 %all-gather.19.cloned.1.call-done = f32[512,4,256]{2,0,1:T(8,128)} async-done(((f32[32,4,256]{2,0,1:T(8,128)}), f32[512,4,256]{2,0,1:T(8,128)}) %all-gather.19.cloned.1.call-update) | async-done | bytes 2097168 | tf_op jit(solution)/shard_map/all_gather | solution.py:42
  537.1 4.9 convolution_bitcast_fusion.3
  542.1 21.7 %all-gather.15.cloned.1.call-done = f32[512,4,256]{2,0,1:T(8,128)} async-done(((f32[64,4,256]{2,0,1:T(8,128)}), f32[512,4,256]{2,0,1:T(8,128)}) %all-gather.15.cloned.1.call-update) | async-done | bytes 2097168 | tf_op jit(solution)/shard_map/all_gather | solution.py:18
  563.8 68.5 %all-reduce.7.cloned.1.call-done = f32[512,4,256]{2,0,1:T(8,128)} async-done(((f32[512,4,256]{2,0,1:T(8,128)}), f32[512,4,256]{2,0,1:T(8,128)}) %all-reduce.7.cloned.1.call-update) | async-done | bytes 2097168 | tf_op jit(solution)/shard_map/psum | solution.py:46
  632.3 7.8 %convolution_bitcast_fusion.1 = f32[512,4,512]{2,0,1:T(8,128)} fusion(f32[4,256,512]{2,1,0:T(8,128)S(1)} %copy-done, f32[512,4,256]{2,0,1:T(8,128)} %all-gather.15.cloned.1.call-done, f32[512,4,256]{2,0,1:T(8,128)} %all-reduce.7.cloned.1.call-done), kind=kOutput, calls=%fused_computation.4 | convolution fusion | flops 3221749760 | bytes 10485760 | tf_op jit(solution)/shard_map/ski,kij->skj/dot_general | solution.py:23
  642.7 74.9 %reduce-scatter.5.cloned.1.call-done = f32[32,4,512]{2,0,1:T(8,128)} async-done(((f32[512,4,512]{2,0,1:T(8,128)}), f32[32,4,512]{2,0,1:T(8,128)}) %reduce-scatter.5.cloned.1.call-update) | async-done | bytes 262160 | tf_op jit(solution)/shard_map/reduce_scatter | solution.py:22
  (68 shorter events, 15.4 us)
Async XLA Ops:
  7.2 625.1 %copy-start = (f32[4,256,512]{2,1,0:T(8,128)S(1)}, f32[4,256,512]{2,1,0:T(8,128)}, u32[]{:S(2)}) copy-start(f32[4,256,512]{2,1,0:T(8,128)} %param.15) | copy-start | bytes 6291460
  7.2 30.2 %all-gather.21.cloned.1.call-start = ((), (), s32[]{:S(2)}) async-start(), calls=%async_computation.12 | async-start | bytes 2359296 | tf_op jit(solution)/shard_map/all_gather | solution.py:18
  7.9 175.0 %all-reduce.9.cloned.1.call-start = ((), (), s32[]{:S(2)}) async-start(), calls=%async_computation.13 | async-start | bytes 8388608
  78.8 0.7 copy-start.8
  78.8 105.9 %copy-start.7 = (s32[2,4]{1,0:T(2,128)S(1)}, s32[2,4]{1,0:T(2,128)}, u32[]{:S(2)}) copy-start(s32[2,4]{1,0:T(2,128)} %param.18) | copy-start | bytes 100
  78.8 131.2 %all-gather.11.cloned.1.call-start = ((), (), s32[]{:S(2)}) async-start(), calls=%async_computation.3 | async-start | bytes 2359296 | tf_op jit(solution)/shard_map/all_gather | solution.py:37
  184.7 78.4 %all-gather.13.cloned.1.call-start = ((), (), s32[]{:S(2)}) async-start(), calls=%async_computation.4 | async-start | bytes 2228224 | tf_op jit(solution)/shard_map/all_gather | solution.py:42
  210.0 7.3 %copy-start.5 = (f32[64,2,512]{2,1,0:T(2,128)S(1)}, f32[64,2,512]{2,1,0:T(2,128)}, u32[]{:S(2)}) copy-start(f32[64,2,512]{2,1,0:T(2,128)} %param.11) | copy-start | bytes 786436
  217.3 72.3 %all-gather.9.cloned.1.call-start = ((), (), s32[]{:S(2)}) async-start(), calls=%async_computation.2 | async-start | bytes 2359296 | tf_op jit(solution)/shard_map/all_gather | solution.py:18
  218.1 139.7 %all-reduce.5.cloned.1.call-start = ((), (), s32[]{:S(2)}) async-start(), calls=%async_computation.5 | async-start | bytes 4194304 | tf_op jit(solution)/shard_map/psum | solution.py:46
  270.1 177.5 %reduce-scatter.3.cloned.1.call-start = ((), (), s32[]{:S(2)}) async-start(), calls=%async_computation.6 | async-start | bytes 4456448 | tf_op jit(solution)/shard_map/reduce_scatter | solution.py:22
  370.0 77.7 %copy-start.6 = (s32[4,2]{0,1:T(2,128)S(1)}, s32[4,2]{0,1:T(2,128)}, u32[]{:S(2)}) copy-start(s32[4,2]{0,1:T(2,128)} %param.19) | copy-start | bytes 100
  370.0 103.7 %all-gather.17.cloned.1.call-start = ((), (), s32[]{:S(2)}) async-start(), calls=%async_computation.8 | async-start | bytes 2359296 | tf_op jit(solution)/shard_map/all_gather | solution.py:37
  447.6 89.6 %all-gather.19.cloned.1.call-start = ((), (), s32[]{:S(2)}) async-start(), calls=%async_computation.9 | async-start | bytes 2228224 | tf_op jit(solution)/shard_map/all_gather | solution.py:42
  482.3 3.0 copy-start.1
  487.7 49.5 %copy-start.3 = (f32[4,256,256]{2,1,0:T(8,128)S(1)}, f32[4,256,256]{2,1,0:T(8,128)}, u32[]{:S(2)}) copy-start(f32[4,256,256]{2,1,0:T(8,128)} %param.17) | copy-start | bytes 3145732
  491.4 72.4 %all-gather.15.cloned.1.call-start = ((), (), s32[]{:S(2)}) async-start(), calls=%async_computation.7 | async-start | bytes 2359296 | tf_op jit(solution)/shard_map/all_gather | solution.py:18
  493.2 139.1 %all-reduce.7.cloned.1.call-start = ((), (), s32[]{:S(2)}) async-start(), calls=%async_computation.10 | async-start | bytes 4194304 | tf_op jit(solution)/shard_map/psum | solution.py:46
  542.0 175.5 %reduce-scatter.5.cloned.1.call-start = ((), (), s32[]{:S(2)}) async-start(), calls=%async_computation.11 | async-start | bytes 4456448 | tf_op jit(solution)/shard_map/reduce_scatter | solution.py:22
  640.0 0.9 copy-start.2
  640.0 1.7 copy-start.4
Sparse Core Ops, SparseCore 0:
  9.7 27.5 all-gather.20
  79.0 103.9 all-reduce.8
  185.2 24.7 all-gather.10
  217.4 45.5 all-gather.12
  265.2 24.3 all-gather.8
  291.8 65.9 all-reduce.4
  370.1 77.3 reduce-scatter.2
  449.4 24.3 all-gather.16
  491.5 45.5 all-gather.18
  539.4 24.3 all-gather.14
  566.3 65.9 all-reduce.6
  640.2 77.3 reduce-scatter.4
where the time goes:
time: 727 us; the launch traced here: 726 us
  waiting for transfers between devices  602 us (83%)
  matrix products  62.3 us (9%)
  local copies, waits for them, and re-layouts  42.2 us (6%)
  between operations  15 us (2%)
    reduce_scatter x2, waiting for transfers between devices, solve_terms(): lax.psum_scatter(jnp.einsum('ski,kij->skj', right_rows, inverse, precisio...  152 us
    psum x2, waiting for transfers between devices, finish_level(): summed = lax.psum(partial_value, 'col')  137 us
    unnamed x13, waiting for transfers between devices  103 us
    all_gather x2, waiting for transfers between devices, fetch_ancestors(): lax.all_gather(pick_blocks(source_rows, blocks), 'wide', axis=0, tiled=True)  88.8 us
    all_gather x3, waiting for transfers between devices, spread_rhs(): return lax.all_gather(local_part, 'col', axis=0, tiled=True)  70.5 us
    all_gather x2, waiting for transfers between devices, spread_solved(): gathered = lax.all_gather(solved_local, 'col', axis=2, tiled=True)  50.9 us
    dot_general x3, matrix products, solve_terms(): jnp.einsum('ski,kij->skj', right_rows, inverse, precision=PRECISE, prefer...  50.4 us
  transfers between devices with their start and end apart: 12, of which 12 were waited for; matrix products, arithmetic and copies ran while one was open for 2% of the time, Pallas kernels for 0%

commit v1 on v0

--- a/solution.py
+++ b/solution.py
@@ -39,7 +39,12 @@
 
 
 def fetch_ancestors(source_rows, blocks):
-    return lax.all_gather(pick_blocks(source_rows, blocks), "wide", axis=0, tiled=True)
+    return jnp.concatenate(
+        lax.all_to_all(
+            jnp.stack([pick_blocks(source_rows, blocks)] * lax.axis_size("wide")), "wide", 0, 0
+        ),
+        axis=0,
+    )
 
 
 def finish_level(z_local, inverse, partial_value):

time: 727 us -> 651 us (0.90)
  waiting for transfers between devices: 602 us -> 459 us
  blocking collectives: 0 us -> 71.2 us
    all_gather x2 -> x0, waiting for transfers between devices: 88.8 us -> none  [fetch_ancestors(): lax.all_gather(pick_blocks(source_rows, blocks), 'wide', axis=0, tiled=True)]
    all_to_all x0 -> x2, blocking collectives: none -> 71.2 us  [fetch_ancestors(): lax.all_to_all(jnp.stack([pick_blocks(source_rows, blocks)] * lax.axis_si...]
    all_gather x3, waiting for transfers between devices: 70.5 us -> 29.4 us  [spread_rhs(): return lax.all_gather(local_part, 'col', axis=0, tiled=True)]
    psum x2, waiting for transfers between devices: 137 us -> 124 us  [finish_level(): summed = lax.psum(partial_value, 'col')]
    unnamed x13 -> x11, waiting for transfers between devices: 103 us -> 103 us
  transfers between devices with their start and end apart: 12 -> 10, of which waited for: 12 -> 8; matrix products, arithmetic and copies ran while one was open for 2% -> 6% of each run, Pallas kernels for 0% -> 0%
where the time goes in v1:
time: 651 us
  waiting for transfers between devices  459 us (71%)
  blocking collectives  71.2 us (11%)
  matrix products  58.6 us (9%)
  local copies, waits for them, and re-layouts  44.4 us (7%)
  between operations  15 us (2%)
    reduce_scatter x2, waiting for transfers between devices, solve_terms(): lax.psum_scatter(jnp.einsum('ski,kij->skj', right_rows, inverse, precisio...  152 us
    psum x2, waiting for transfers between devices, finish_level(): summed = lax.psum(partial_value, 'col')  124 us
    unnamed x11, waiting for transfers between devices  103 us
    all_to_all x2, blocking collectives, fetch_ancestors(): lax.all_to_all(jnp.stack([pick_blocks(source_rows, blocks)] * lax.axis_si...  71.2 us
    dot_general x3, matrix products, solve_terms(): jnp.einsum('ski,kij->skj', right_rows, inverse, precision=PRECISE, prefer...  50.4 us
    all_gather x2, waiting for transfers between devices, spread_solved(): gathered = lax.all_gather(solved_local, 'col', axis=2, tiled=True)  49.3 us
    all_gather x3, waiting for transfers between devices, spread_rhs(): return lax.all_gather(local_part, 'col', axis=0, tiled=True)  29.4 us
  transfers between devices with their start and end apart: 10, of which 8 were waited for; matrix products, arithmetic and copies ran while one was open for 6% of the time, Pallas kernels for 0%

profile of v1, /device:TPU:0, one launch (start us, length us, event | category | flops | bytes accessed | tf_op | source)
XLA Modules:
  0.0 650.6 jit_solution(3044809773003770590)
XLA Ops:
  8.0 29.4 %all-gather.15.cloned.1.call-done = f32[512,1024]{1,0:T(8,128)} async-done(((f32[64,1024]{1,0:T(8,128)}), f32[512,1024]{1,0:T(8,128)}) %all-gather.15.cloned.1.call-update) | async-done | bytes 2097168 | tf_op jit(solution)/shard_map/all_gather | solution.py:18
  37.4 30.4 %convolution_bitcast_fusion = f32[512,1,2048]{0,2,1:T(8,128)} fusion(f32[1024,2048]{1,0:T(8,128)} %param.13, f32[512,1024]{1,0:T(8,128)} %all-gather.15.cloned.1.call-done), kind=kOutput, calls=%fused_computation.3 | convolution fusion | flops 12884901888 | bytes 14680064 | tf_op jit(solution)/shard_map/ski,kij->skj/dot_general | solution.py:23
  67.8 11.0 %copy.79 = f32[512,1,2048]{2,1,0:T(1,128)} copy(f32[512,1,2048]{0,2,1:T(8,128)} %convolution_bitcast_fusion) | data formatting | bytes 8388608 | tf_op jit(solution)/shard_map/ski,kij->skj/transpose | solution.py:23
  80.7 102.3 %all-reduce.9.cloned.1.call-done = f32[512,1,2048]{2,1,0:T(1,128)} async-done(((f32[512,1,2048]{2,1,0:T(1,128)}), f32[512,1,2048]{2,1,0:T(1,128)}) %all-reduce.9.cloned.1.call-update) | async-done | bytes 4194320
  185.8 24.3 %all-gather.9.cloned.1.call-done = f32[32,1,16384]{2,1,0:T(1,128)} async-done(((f32[32,1,2048]{2,1,0:T(1,128)}), f32[32,1,16384]{2,1,0:T(1,128)}) %all-gather.9.cloned.1.call-update) | async-done | bytes 2097168 | tf_op jit(solution)/shard_map/all_gather | solution.py:37
  210.1 4.2 copy.81
  214.2 2.1 gather_fusion
  216.9 35.6 %all_to_all.10 = f32[16,32,2,512]{3,1,2,0:T(8,128)S(1)} all-to-all(f32[16,32,2,512]{3,1,2,0:T(8,128)S(1)} %stack.6), channel_id=1, replica_groups=mesh['wide'=16,'col'=8] {'wide'}, dimensions={0} | all-to-all | bytes 4194304 | tf_op jit(solution)/shard_map/all_to_all | solution.py:43
  254.1 4.8 convolution_bitcast_fusion.4
  259.0 62.1 %all-reduce.5.cloned.1.call-done = f32[512,2,512]{2,0,1:T(8,128)} async-done(((f32[512,2,512]{2,0,1:T(8,128)}), f32[512,2,512]{2,0,1:T(8,128)}) %all-reduce.5.cloned.1.call-update) | async-done | bytes 2097168 | tf_op jit(solution)/shard_map/psum | solution.py:51
  321.1 12.2 %convolution_bitcast_fusion.2 = f32[512,2,1024]{2,0,1:T(8,128)} fusion(f32[2,512,1024]{2,1,0:T(8,128)} %param.14, f32[512,2,512]{2,0,1:T(8,128)} %all-gather.7.cloned.1.call-done, f32[512,2,512]{2,0,1:T(8,128)} %all-reduce.5.cloned.1.call-done), kind=kOutput, calls=%fused_computation.5 | convolution fusion | flops 6442975232 | bytes 12582912 | tf_op jit(solution)/shard_map/ski,kij->skj/dot_general | solution.py:23
  333.4 77.5 %reduce-scatter.3.cloned.1.call-done = f32[32,2,1024]{2,0,1:T(8,128)} async-done(((f32[512,2,1024]{2,0,1:T(8,128)}), f32[32,2,1024]{2,0,1:T(8,128)}) %reduce-scatter.3.cloned.1.call-update) | async-done | bytes 262160 | tf_op jit(solution)/shard_map/reduce_scatter | solution.py:22
  412.1 25.0 %all-gather.13.cloned.1.call-done = f32[32,2,8192]{2,0,1:T(8,128)} async-done(((f32[32,2,1024]{2,0,1:T(8,128)}), f32[32,2,8192]{2,0,1:T(8,128)}) %all-gather.13.cloned.1.call-update) | async-done | bytes 2097168 | tf_op jit(solution)/shard_map/all_gather | solution.py:37
  437.1 4.5 copy.86
  441.6 4.0 concatenate.6
  445.6 3.0 copy.88
  448.6 2.4 pad_maximum_fusion
  451.0 2.7 gather_fusion.1
  454.2 35.6 %all_to_all.11 = f32[16,32,4,256]{3,1,2,0:T(8,128)S(1)} all-to-all(f32[16,32,4,256]{3,1,2,0:T(8,128)S(1)} %stack.7), channel_id=1, replica_groups=mesh['wide'=16,'col'=8] {'wide'}, dimensions={0} | all-to-all | bytes 4194304 | tf_op jit(solution)/shard_map/all_to_all | solution.py:43
  491.0 3.3 convolution_bitcast_fusion.3
  494.5 62.1 %all-reduce.7.cloned.1.call-done = f32[512,4,256]{2,0,1:T(8,128)} async-done(((f32[512,4,256]{2,0,1:T(8,128)}), f32[512,4,256]{2,0,1:T(8,128)}) %all-reduce.7.cloned.1.call-update) | async-done | bytes 2097168 | tf_op jit(solution)/shard_map/psum | solution.py:51
  556.6 7.7 %convolution_bitcast_fusion.1 = f32[512,4,512]{2,0,1:T(8,128)} fusion(f32[4,256,512]{2,1,0:T(8,128)S(1)} %copy-done, f32[512,4,256]{2,0,1:T(8,128)} %all-gather.11.cloned.1.call-done, f32[512,4,256]{2,0,1:T(8,128)} %all-reduce.7.cloned.1.call-done), kind=kOutput, calls=%fused_computation.4 | convolution fusion | flops 3221749760 | bytes 10485760 | tf_op jit(solution)/shard_map/ski,kij->skj/dot_general | solution.py:23
  567.0 75.0 %reduce-scatter.5.cloned.1.call-done = f32[32,4,512]{2,0,1:T(8,128)} async-done(((f32[512,4,512]{2,0,1:T(8,128)}), f32[32,4,512]{2,0,1:T(8,128)}) %reduce-scatter.5.cloned.1.call-update) | async-done | bytes 262160 | tf_op jit(solution)/shard_map/reduce_scatter | solution.py:22
  642.0 1.8 copy.94
  (74 shorter events, 12.5 us)
Async XLA Ops:
  7.2 549.4 %copy-start = (f32[4,256,512]{2,1,0:T(8,128)S(1)}, f32[4,256,512]{2,1,0:T(8,128)}, u32[]{:S(2)}) copy-start(f32[4,256,512]{2,1,0:T(8,128)} %param.15) | copy-start | bytes 6291460
  7.2 30.2 %all-gather.15.cloned.1.call-start = ((), (), s32[]{:S(2)}) async-start(), calls=%async_computation.12 | async-start | bytes 2359296 | tf_op jit(solution)/shard_map/all_gather | solution.py:18
  7.9 175.1 %all-reduce.9.cloned.1.call-start = ((), (), s32[]{:S(2)}) async-start(), calls=%async_computation.13 | async-start | bytes 8388608
  78.8 0.7 copy-start.10
  78.8 105.9 %copy-start.6 = (f32[64,2,512]{2,1,0:T(2,128)S(1)}, f32[64,2,512]{2,1,0:T(2,128)}, u32[]{:S(2)}) copy-start(f32[64,2,512]{2,1,0:T(2,128)} %param.11) | copy-start | bytes 786436
  78.8 106.7 %copy-start.9 = (s32[2,4]{1,0:T(2,128)S(1)}, s32[2,4]{1,0:T(2,128)}, u32[]{:S(2)}) copy-start(s32[2,4]{1,0:T(2,128)} %param.18) | copy-start | bytes 100
  78.9 131.2 %all-gather.9.cloned.1.call-start = ((), (), s32[]{:S(2)}) async-start(), calls=%async_computation.5 | async-start | bytes 2359296 | tf_op jit(solution)/shard_map/all_gather | solution.py:37
  184.7 74.3 %all-gather.7.cloned.1.call-start = ((), (), s32[]{:S(2)}) async-start(), calls=%async_computation.4 | async-start | bytes 2359296 | tf_op jit(solution)/shard_map/all_gather | solution.py:18
  185.5 135.6 %all-reduce.5.cloned.1.call-start = ((), (), s32[]{:S(2)}) async-start(), calls=%async_computation.6 | async-start | bytes 4194304 | tf_op jit(solution)/shard_map/psum | solution.py:51
  252.5 1.6 copy-start.3
  258.9 152.0 %reduce-scatter.3.cloned.1.call-start = ((), (), s32[]{:S(2)}) async-start(), calls=%async_computation.7 | async-start | bytes 4456448 | tf_op jit(solution)/shard_map/reduce_scatter | solution.py:22
  333.3 77.7 %copy-start.7 = (f32[64,4,256]{2,1,0:T(4,128)S(1)}, f32[64,4,256]{2,1,0:T(4,128)}, u32[]{:S(2)}) copy-start(f32[64,4,256]{2,1,0:T(4,128)} %param.12) | copy-start | bytes 786436
  333.3 78.5 %copy-start.8 = (s32[4,2]{0,1:T(2,128)S(1)}, s32[4,2]{0,1:T(2,128)}, u32[]{:S(2)}) copy-start(s32[4,2]{0,1:T(2,128)} %param.19) | copy-start | bytes 100
  333.4 103.8 %all-gather.13.cloned.1.call-start = ((), (), s32[]{:S(2)}) async-start(), calls=%async_computation.9 | async-start | bytes 2359296 | tf_op jit(solution)/shard_map/all_gather | solution.py:37
  410.9 83.5 %all-gather.11.cloned.1.call-start = ((), (), s32[]{:S(2)}) async-start(), calls=%async_computation.8 | async-start | bytes 2359296 | tf_op jit(solution)/shard_map/all_gather | solution.py:18
  411.8 144.8 %all-reduce.7.cloned.1.call-start = ((), (), s32[]{:S(2)}) async-start(), calls=%async_computation.10 | async-start | bytes 4194304 | tf_op jit(solution)/shard_map/psum | solution.py:51
  445.6 3.0 copy-start.1
  489.8 1.2 copy-start.4
  494.4 147.6 %reduce-scatter.5.cloned.1.call-start = ((), (), s32[]{:S(2)}) async-start(), calls=%async_computation.11 | async-start | bytes 4456448 | tf_op jit(solution)/shard_map/reduce_scatter | solution.py:22
  564.4 0.9 copy-start.2
  564.4 1.7 copy-start.5
Sparse Core Ops, SparseCore 0:
  9.7 27.5 all-gather.14
  79.0 103.9 all-reduce.8
  185.2 24.7 all-gather.8
  212.2 25.4 all-gather.6
  259.1 62.0 all-reduce.4
  333.5 77.3 reduce-scatter.2
  412.7 24.3 all-gather.12
  439.5 25.4 all-gather.10
  494.5 62.0 all-reduce.6
  564.5 77.4 reduce-scatter.4
